TPU v7x, 256 devices: a whole 4x4x8 slice. The times are simulated.
256 devices in a mesh: dp: 8 (over x, z_hi), ctx: 32 (over z_lo, y, core).
Axes of the slice: x: 4, y: 4, z: 8 (z_hi: 2, z_lo: 4; z = z_hi * 4 + z_lo), core: 2. Of those that a mesh axis runs over, the one named last changes fastest.
Arguments:
- queries: bfloat16 [32768, 1024], P(('dp', 'ctx')), parts along dimension 0, may hold values from -8 to 8
- keys: bfloat16 [32768, 1024], P(('dp', 'ctx')), parts along dimension 0, may hold values from -8 to 8
- values: bfloat16 [32768, 1024], P(('dp', 'ctx')), parts along dimension 0, may hold values from -6 to 6
- grad_out: bfloat16 [32768, 1024], P(('dp', 'ctx')), parts along dimension 0, may hold values from -6 to 6
- rand_blocks: int32 [512, 3], P(('dp', 'ctx')), parts along dimension 0, may hold values from 0 to 1
- global_ids: int32 [16], P('dp'), parts along dimension 0, may hold values from 0 to 63
Outputs:
- attended: bfloat16 [32768, 1024], P(('dp', 'ctx')), parts along dimension 0
- grad_queries: bfloat16 [32768, 1024], P(('dp', 'ctx')), parts along dimension 0
- grad_keys: bfloat16 [32768, 1024], P(('dp', 'ctx')), parts along dimension 0
- grad_values: bfloat16 [32768, 1024], P(('dp', 'ctx')), parts along dimension 0
There are 8 independent parts, one for each index of `dp`. A program takes and returns all parts, laid end to end along the dimension named above; each array names one. Nothing has to cross between parts.
All inputs are finite; a program needn't handle non-finite values.
Results may differ from a plain program's by a relative error of at most 0.02.
Values may be sent and summed in bfloat16 or wider, within the bound.
No kernel may reach another device: no remote copies, remote signals or barrier semaphores. Data moves between devices by JAX's collectives and lax.ppermute only.
A program may use at most 128 MiB of HBM per device.

v0:
```python
import jax
import jax.numpy as jnp
from jax import lax
from jax.sharding import PartitionSpec as P

HEADS = 16
HEAD_DIM = 64
BLOCK = 64
RAND = 3
GLOBALS = 2
SCORE_FLOOR = -1e30


def padded_2(array, sides, width):
    for axis, dim in sides:
        size, length = (lax.axis_size(axis), array.shape[dim])
        up = [(i, (i + 1) % size) for i in range(size - 1)]
        down = [(j, i) for i, j in up]
        last = lax.slice_in_dim(array, length - width, length, axis=dim)
        first = lax.slice_in_dim(array, 0, width, axis=dim)
        before = lax.ppermute(last, axis, up)
        after = lax.ppermute(first, axis, down)
        array = jnp.concatenate([before, array, after], axis=dim)
    return array


def from_root(block, axis, source):
    block = jnp.where(lax.axis_index(axis) == source, block, jnp.zeros_like(block))
    return lax.psum(block, axis)


def partner_2(array, axis, distance):
    return lax.ppermute(array, axis, [(i, i ^ 1 << distance) for i in range(lax.axis_size(axis))])


def passed_along(array, axis, by):
    size = lax.axis_size(axis)
    pairs = [(i, i + by) for i in range(size) if 0 <= i + by < size]
    return lax.ppermute(array, axis, pairs)


def attend_blocks(query_blocks, key_blocks, value_blocks, grad_blocks, key_valid):
    scale_factor = HEAD_DIM ** (-0.5)
    scores = (
        jnp.einsum("jqhd,jkhd->jhqk", query_blocks, key_blocks, preferred_element_type=jnp.float32)
        * scale_factor
    )
    scores = jnp.where(key_valid[:, None, None, :], scores, SCORE_FLOOR)
    highest = jnp.max(scores, axis=-1, keepdims=True)
    raw_weights = jnp.exp(scores - highest)
    weight_total = jnp.sum(raw_weights, axis=-1, keepdims=True)
    probs = raw_weights / weight_total
    probs_low = probs.astype(jnp.bfloat16)
    attended = jnp.einsum(
        "jhqk,jkhd->jqhd", probs_low, value_blocks, preferred_element_type=jnp.float32
    )
    grad_probs = jnp.einsum(
        "jqhd,jkhd->jhqk", grad_blocks, value_blocks, preferred_element_type=jnp.float32
    )
    inner = jnp.sum(probs * grad_probs, axis=-1, keepdims=True)
    grad_scores = (scale_factor * probs * (grad_probs - inner)).astype(jnp.bfloat16)
    grad_query = jnp.einsum(
        "jhqk,jkhd->jqhd", grad_scores, key_blocks, preferred_element_type=jnp.float32
    )
    grad_key = jnp.einsum(
        "jhqk,jqhd->jkhd", grad_scores, query_blocks, preferred_element_type=jnp.float32
    )
    grad_value = jnp.einsum(
        "jhqk,jqhd->jkhd", probs_low, grad_blocks, preferred_element_type=jnp.float32
    )
    return (attended, grad_query, grad_key, grad_value, (highest, weight_total, inner))


def local(queries, keys, values, grad_out, rand_blocks, global_ids):
    tok_rows, width = queries.shape
    block_count = tok_rows // BLOCK
    listed = 3 + GLOBALS + RAND
    ctx_count = lax.axis_size("ctx")
    position = lax.axis_index("ctx")
    top_bit = ctx_count.bit_length() - 1
    block_iota = jnp.arange(block_count, dtype=jnp.int32)
    stacked = jnp.stack([keys, values])
    padded = padded_2(stacked, (("ctx", 1),), BLOCK)
    framed = padded.reshape(2, block_count + 2, BLOCK, width)
    window = jnp.concatenate([framed[:, :-2], framed[:, 1:-1], framed[:, 2:]], axis=2)
    owners = global_ids // block_count
    local_ids = global_ids % block_count
    own_pieces = jnp.stack(
        [
            lax.dynamic_slice_in_dim(stacked, local_ids[global_slot] * BLOCK, BLOCK, 1)
            for global_slot in range(GLOBALS)
        ],
        axis=1,
    )
    fetched = jnp.stack(
        [
            from_root(own_pieces[:, global_slot], "ctx", owners[global_slot])
            for global_slot in range(GLOBALS)
        ],
        axis=1,
    )
    global_part = jnp.broadcast_to(
        fetched.reshape(2, 1, GLOBALS * BLOCK, width), (2, block_count, GLOBALS * BLOCK, width)
    )
    pickers = []
    random_parts = []
    for matching in range(RAND):
        spread_bit = top_bit - 1 - matching
        picker = (rand_blocks[:, matching][:, None] == block_iota[None, :]).astype(jnp.bfloat16)
        partner = partner_2(stacked, "ctx", spread_bit).reshape(2, block_count, BLOCK, width)
        chosen = jnp.einsum(
            "jb,sbqd->sjqd", picker, partner, preferred_element_type=jnp.float32
        ).astype(jnp.bfloat16)
        pickers.append(picker)
        random_parts.append(chosen)
    every_key = jnp.concatenate([window, global_part] + random_parts, axis=2)
    key_blocks = every_key[0].reshape(block_count, listed * BLOCK, HEADS, HEAD_DIM)
    value_blocks = every_key[1].reshape(block_count, listed * BLOCK, HEADS, HEAD_DIM)
    global_block = position * block_count + block_iota
    seq_blocks = block_count * ctx_count
    left_ok = global_block > 0
    right_ok = global_block < seq_blocks - 1
    key_valid = jnp.concatenate(
        [
            jnp.broadcast_to(left_ok[:, None], (block_count, BLOCK)),
            jnp.ones((block_count, BLOCK), dtype=bool),
            jnp.broadcast_to(right_ok[:, None], (block_count, BLOCK)),
            jnp.ones((block_count, (GLOBALS + RAND) * BLOCK), dtype=bool),
        ],
        axis=1,
    )
    query_blocks = queries.reshape(block_count, BLOCK, HEADS, HEAD_DIM)
    grad_blocks = grad_out.reshape(block_count, BLOCK, HEADS, HEAD_DIM)
    attended, grad_query, grad_key, grad_value, softmax_stats = attend_blocks(
        query_blocks, key_blocks, value_blocks, grad_blocks, key_valid
    )
    split = jnp.stack([grad_key, grad_value]).reshape(2, block_count, listed, BLOCK, width)
    own_window = (
        jnp.pad(split[:, :, 0], ((0, 0), (0, 2), (0, 0), (0, 0)))
        + jnp.pad(split[:, :, 1], ((0, 0), (1, 1), (0, 0), (0, 0)))
        + jnp.pad(split[:, :, 2], ((0, 0), (2, 0), (0, 0), (0, 0)))
    )
    from_right = passed_along(own_window[:, 0], "ctx", -1)
    from_left = passed_along(own_window[:, -1], "ctx", 1)
    own_total = own_window[:, 1:-1]
    own_total = own_total.at[:, -1].add(from_right)
    own_total = own_total.at[:, 0].add(from_left)
    for matching in range(RAND):
        spread_bit = top_bit - 1 - matching
        terms = split[:, :, 3 + GLOBALS + matching]
        routed = jnp.einsum(
            "jb,sjqd->sbqd",
            pickers[matching].astype(jnp.float32),
            terms,
            precision=lax.Precision.HIGHEST,
        )
        own_total = own_total + partner_2(routed, "ctx", spread_bit)
    attended_out = attended.reshape(tok_rows, width).astype(jnp.bfloat16)
    grad_queries = grad_query.reshape(tok_rows, width).astype(jnp.bfloat16)
    grad_keys = own_total[0].reshape(tok_rows, width).astype(jnp.bfloat16)
    grad_values = own_total[1].reshape(tok_rows, width).astype(jnp.bfloat16)
    return (attended_out, grad_queries, grad_keys, grad_values)


def solution(mesh):
    placed = (
        P(("dp", "ctx"), None),
        P(("dp", "ctx"), None),
        P(("dp", "ctx"), None),
        P(("dp", "ctx"), None),
        P(("dp", "ctx"), None),
        P("dp"),
    )
    return jax.shard_map(
        local,
        mesh=mesh,
        in_specs=placed,
        out_specs=(
            P(("dp", "ctx"), None),
            P(("dp", "ctx"), None),
            P(("dp", "ctx"), None),
            P(("dp", "ctx"), None),
        ),
        check_vma=False,
    )
```

profile of v0, /device:TPU:96, one launch (start us, length us, event | category | flops | bytes accessed | tf_op | source)
XLA Modules:
  0.0 459.5 jit_solution(9011491721710918860)
XLA Ops:
  7.3 1.9 pad_maximum_fusion.2
  9.2 3.2 collective-permute-start.4
  16.4 2.2 fusion.34
  18.6 1.9 collective-permute-start
  20.5 5.8 %collective-permute-start.1 = (bf16[2,64,1024]{2,1,0:T(8,128)(2,1)S(1)}, bf16[2,64,1024]{2,1,0:T(8,128)(2,1)S(1)}, u32[]{:S(2)}, u32[]{:S(2)}) collective-permute-start(bf16[2,64,1024]{2,1,0:T(8,128)(2,1)S(1)} %get-tuple-element.48), channel_id=1, source_target_pairs={{1,0},{2,1},{3,2},{4,3},{5,4},{6,5},{7,6},{8,7},{9,8},{10,9},{11,1... | collective-permute-start | bytes 786440 | tf_op jit(solution)/shard_map/ppermute | solution.py:22
  26.5 1.3 reshape.131
  29.5 1.3 copy.51
  31.1 9.4 %collective-permute-done = bf16[2,64,1024]{2,1,0:T(8,128)(2,1)S(1)} collective-permute-done((bf16[2,64,1024]{2,1,0:T(8,128)(2,1)S(1)}, bf16[2,64,1024]{2,1,0:T(8,128)(2,1)S(1)}, u32[]{:S(2)}, u32[]{:S(2)}) %collective-permute-start) | collective-permute-done | bytes 262176 | tf_op jit(solution)/shard_map/ppermute | solution.py:21
  42.6 1.5 copy.75
  44.1 2.6 fusion.15
  46.7 2.3 copy.44
  49.0 2.6 fusion.13
  51.6 2.3 copy.42
  53.9 2.6 fusion.14
  56.5 2.3 copy.43
  58.8 234.1 %all-reduce.6.cloned.1.call-done = (bf16[2,1,64,1024]{3,2,1,0:T(8,128)(2,1)}, bf16[2,1,64,1024]{3,2,0,1:T(8,128)(2,1)}) async-done(((bf16[2,1,64,1024]{3,2,1,0:T(8,128)(2,1)}, bf16[2,1,64,1024]{3,2,0,1:T(8,128)(2,1)}), (bf16[2,1,64,1024]{3,2,1,0:T(8,128)(2,1)}, bf16[2,1,64,1024]{3,2,0,1:T(8,128)(2,1)})) %all-reduce.6.cloned.1.call-update) | async-done | bytes 524304 | tf_op jit(solution)/shard_map/psum | solution.py:29
  292.9 1.9 pad_maximum_fusion.3
  294.8 2.1 copy.35
  296.9 2.2 broadcast_in_dim.25
  299.1 10.3 %concatenate.15 = bf16[2,2,512,1024]{2,3,1,0:T(8,128)(2,1)} concatenate(bf16[2,2,64,1024]{2,3,1,0:T(8,128)(2,1)S(1)} %copy.75, bf16[2,2,64,1024]{2,3,1,0:T(8,128)(2,1)S(1)} %copy.76, bf16[2,2,64,1024]{2,3,1,0:T(8,128)(2,1)S(1)} %copy.77, bf16[2,2,128,1024]{2,3,1,0:T(8,128)(2,1)} %broadcast_in_dim.25, bf16[2,2,64,1024]{2,3,1,0:T(8,128)(2,1)} %copy.42, ...), dimensions={2} | concatenate | bytes 8388608 | tf_op jit(solution)/shard_map/concatenate | solution.py:116
  309.4 4.0 fusion.51
  313.4 3.4 fusion.57
  316.8 5.0 %convolution_bitcast_fusion = f32[2,512,16,64]{1,3,2,0:T(8,128)} fusion(bf16[2,64,16,64]{1,3,2,0:T(8,128)(2,1)S(1)} %copy-done.10, f32[2,16,64,512]{3,2,1,0:T(8,128)} %get-tuple-element.57, f32[2,16,64]{2,1,0:T(8,128)S(1)} %get-tuple-element.56), kind=kOutput, calls=%fused_computation.11 | convolution fusion | flops 136314880 | bytes 8658944 | tf_op jit(solution)/shard_map/jhqk,jqhd->jkhd/dot_general | solution.py:68
  324.1 2.6 convolution_bitcast_fusion.1
  326.8 7.1 %reshape.141 = f32[1,2,8,64,1024]{3,2,4,1,0:T(8,128)} reshape(f32[2,512,16,64]{1,3,2,0:T(8,128)} %convolution_bitcast_fusion.1) | data formatting | bytes 8388608 | tf_op jit(solution)/shard_map/stack | solution.py:137
  333.8 8.6 %copy.53 = f32[1,2,8,64,1024]{4,1,3,0,2:T(2,128)} copy(f32[1,2,8,64,1024]{3,2,4,1,0:T(8,128)} %reshape.141) | data formatting | bytes 8388608 | tf_op jit(solution)/shard_map/stack | solution.py:137
  342.5 7.1 %reshape.142 = f32[1,2,8,64,1024]{3,2,4,1,0:T(8,128)} reshape(f32[2,512,16,64]{1,3,2,0:T(8,128)} %convolution_bitcast_fusion) | data formatting | bytes 8388608 | tf_op jit(solution)/shard_map/stack | solution.py:137
  349.6 8.6 %copy.54 = f32[1,2,8,64,1024]{4,1,3,0,2:T(2,128)} copy(f32[1,2,8,64,1024]{3,2,4,1,0:T(8,128)} %reshape.142) | data formatting | bytes 8388608 | tf_op jit(solution)/shard_map/stack | solution.py:137
  358.2 3.6 fusion.20
  362.0 2.3 fusion.19
  364.3 2.3 fusion.21
  366.7 1.7 maximum_bitcast_fusion.4
  369.6 1.3 copy.97
  372.2 1.3 pad_add_fusion
  373.6 2.1 fusion.52
  376.5 1.9 collective-permute-start.5
  378.4 8.8 %collective-permute-start.9 = (f32[2,2,64,1024]{3,2,0,1:T(8,128)}, f32[2,2,64,1024]{3,2,0,1:T(8,128)}, u32[]{:S(2)}, u32[]{:S(2)}) collective-permute-start(f32[2,2,64,1024]{3,2,0,1:T(8,128)} %bitcast.128), channel_id=1, source_target_pairs={{0,4},{1,5},{2,6},{3,7},{4,0},{5,1},{6,2},{7,3},{8,12},{9,13},{10,... | collective-permute-start | bytes 3145736 | tf_op jit(solution)/shard_map/ppermute | solution.py:33
  387.2 5.5 %collective-permute-start.8 = (f32[2,2,64,1024]{3,2,0,1:T(8,128)}, f32[2,2,64,1024]{3,2,0,1:T(8,128)}, u32[]{:S(2)}, u32[]{:S(2)}) collective-permute-start(f32[2,2,64,1024]{3,2,0,1:T(8,128)} %bitcast.129), channel_id=1, source_target_pairs={{0,8},{1,9},{2,10},{3,11},{4,12},{5,13},{6,14},{7,15},{8,0},{9,1},... | collective-permute-start | bytes 3145736 | tf_op jit(solution)/shard_map/ppermute | solution.py:33
  392.8 1.6 fusion.11
  395.0 2.3 copy.46
  397.2 2.1 convert_element_type.71
  399.4 2.0 copy.99
  401.3 2.5 collective-permute-start.6
  403.8 3.1 fusion.12
  406.9 1.5 copy.48
  409.8 1.3 fusion.24
  411.1 37.3 %collective-permute-done.6 = f32[2,64,1024]{2,1,0:T(8,128)} collective-permute-done((f32[2,64,1024]{2,1,0:T(8,128)}, f32[2,64,1024]{2,1,0:T(8,128)}, u32[]{:S(2)}, u32[]{:S(2)}) %collective-permute-start.6) | collective-permute-done | bytes 524320 | tf_op jit(solution)/shard_map/ppermute | solution.py:39
  449.6 2.2 add_convert_fusion
  (66 shorter events, 15.5 us)
Async XLA Ops:
  7.2 33.4 %copy-start.6 = (bf16[128,1024]{1,0:T(8,128)(2,1)S(1)}, bf16[128,1024]{1,0:T(8,128)(2,1)}, u32[]{:S(2)}) copy-start(bf16[128,1024]{1,0:T(8,128)(2,1)} %param.12) | copy-start | bytes 786436
  7.2 33.3 %copy-start.5 = (bf16[128,1024]{1,0:T(8,128)(2,1)S(1)}, bf16[128,1024]{1,0:T(8,128)(2,1)}, u32[]{:S(2)}) copy-start(bf16[128,1024]{1,0:T(8,128)(2,1)} %param.11) | copy-start | bytes 786436
  7.2 21.9 %copy-start.11 = (bf16[128,1024]{1,0:T(8,128)(2,1)S(1)}, bf16[128,1024]{1,0:T(8,128)(2,1)}, u32[]{:S(2)}) copy-start(bf16[128,1024]{1,0:T(8,128)(2,1)} %param.13) | copy-start | bytes 786436
  7.2 23.7 %copy-start.12 = (s32[2,3]{1,0:T(2,128)S(1)}, s32[2,3]{1,0:T(2,128)}, u32[]{:S(2)}) copy-start(s32[2,3]{1,0:T(2,128)} %param.14) | copy-start | bytes 76
  7.2 285.7 %all-reduce.6.cloned.1.call-start = ((), (), s32[]{:S(2)}) async-start(), calls=%async_computation | async-start | bytes 1048576 | tf_op jit(solution)/shard_map/psum | solution.py:29
  9.2 34.9 %collective-permute-start.4 = (bf16[2,128,1024]{2,1,0:T(8,128)(2,1)}, bf16[2,128,1024]{2,1,0:T(8,128)(2,1)}, u32[]{:S(2)}, u32[]{:S(2)}) collective-permute-start(bf16[2,128,1024]{2,1,0:T(8,128)(2,1)} %pad_maximum_fusion.2), channel_id=1, source_target_pairs={{0,4},{1,5},{2,6},{3,7},{4,0},{5,1},{6,2},{7,3},{8,12},{9,13},{10,... | collective-permute-start | bytes 1572872 | tf_op jit(solution)/shard_map/ppermute | solution.py:33
  12.4 36.6 %collective-permute-start.2 = (bf16[2,128,1024]{2,1,0:T(8,128)(2,1)}, bf16[2,128,1024]{2,1,0:T(8,128)(2,1)}, u32[]{:S(2)}, u32[]{:S(2)}) collective-permute-start(bf16[2,128,1024]{2,1,0:T(8,128)(2,1)} %pad_maximum_fusion.2), channel_id=1, source_target_pairs={{0,16},{1,17},{2,18},{3,19},{4,20},{5,21},{6,22},{7,23},{8,24},{9,... | collective-permute-start | bytes 1572872 | tf_op jit(solution)/shard_map/ppermute | solution.py:33
  12.4 41.5 %collective-permute-start.3 = (bf16[2,128,1024]{2,1,0:T(8,128)(2,1)}, bf16[2,128,1024]{2,1,0:T(8,128)(2,1)}, u32[]{:S(2)}, u32[]{:S(2)}) collective-permute-start(bf16[2,128,1024]{2,1,0:T(8,128)(2,1)} %pad_maximum_fusion.2), channel_id=1, source_target_pairs={{0,8},{1,9},{2,10},{3,11},{4,12},{5,13},{6,14},{7,15},{8,0},{9,1},... | collective-permute-start | bytes 1572872 | tf_op jit(solution)/shard_map/ppermute | solution.py:33
  18.6 21.9 %collective-permute-start = (bf16[2,64,1024]{2,1,0:T(8,128)(2,1)S(1)}, bf16[2,64,1024]{2,1,0:T(8,128)(2,1)S(1)}, u32[]{:S(2)}, u32[]{:S(2)}) collective-permute-start(bf16[2,64,1024]{2,1,0:T(8,128)(2,1)S(1)} %get-tuple-element.47), channel_id=1, source_target_pairs={{0,1},{1,2},{2,3},{3,4},{4,5},{5,6},{6,7},{7,8},{8,9},{9,10},{10,1... | collective-permute-start | bytes 786440 | tf_op jit(solution)/shard_map/ppermute | solution.py:21
  20.5 20.0 %collective-permute-start.1 = (bf16[2,64,1024]{2,1,0:T(8,128)(2,1)S(1)}, bf16[2,64,1024]{2,1,0:T(8,128)(2,1)S(1)}, u32[]{:S(2)}, u32[]{:S(2)}) collective-permute-start(bf16[2,64,1024]{2,1,0:T(8,128)(2,1)S(1)} %get-tuple-element.48), channel_id=1, source_target_pairs={{1,0},{2,1},{3,2},{4,3},{5,4},{6,5},{7,6},{8,7},{9,8},{10,9},{11,1... | collective-permute-start | bytes 786440 | tf_op jit(solution)/shard_map/ppermute | solution.py:22
  309.4 4.0 copy-start.9
  313.4 8.4 %copy-start.2 = (bf16[1,2,512,1024]{2,3,1,0:T(8,128)(2,1)}, bf16[1,2,512,1024]{2,3,1,0:T(8,128)(2,1)S(1)}, u32[]{:S(2)}) copy-start(bf16[1,2,512,1024]{2,3,1,0:T(8,128)(2,1)S(1)} %get-tuple-element.36) | copy-start | bytes 6291460
  313.4 3.4 copy-start.10
  316.8 5.0 %copy-start.3 = (f32[2,16,64,512]{3,2,1,0:T(8,128)S(1)}, f32[2,16,64,512]{3,2,1,0:T(8,128)}, u32[]{:S(2)}) copy-start(f32[2,16,64,512]{3,2,1,0:T(8,128)} %get-tuple-element.57) | copy-start | bytes 12582916
  316.8 5.0 %copy-start.7 = (bf16[1,2,512,1024]{2,3,1,0:T(8,128)(2,1)S(1)}, bf16[1,2,512,1024]{2,3,1,0:T(8,128)(2,1)}, u32[]{:S(2)}) copy-start(bf16[1,2,512,1024]{2,3,1,0:T(8,128)(2,1)} %get-tuple-element.37) | copy-start | bytes 6291460
  358.2 3.6 copy-start
  358.2 3.8 copy-start.1
  372.2 20.6 %copy-start.4 = (f32[2,16,64,512]{3,2,1,0:T(8,128)S(1)}, f32[2,16,64,512]{3,2,1,0:T(8,128)}, u32[]{:S(2)}) copy-start(f32[2,16,64,512]{3,2,1,0:T(8,128)} %get-tuple-element.57) | copy-start | bytes 12582916
  372.2 20.6 %copy-start.8 = (bf16[1,2,512,1024]{2,3,1,0:T(8,128)(2,1)S(1)}, bf16[1,2,512,1024]{2,3,1,0:T(8,128)(2,1)}, u32[]{:S(2)}) copy-start(bf16[1,2,512,1024]{2,3,1,0:T(8,128)(2,1)} %get-tuple-element.37) | copy-start | bytes 6291460
  376.5 33.3 %collective-permute-start.5 = (f32[2,64,1024]{2,1,0:T(8,128)}, f32[2,64,1024]{2,1,0:T(8,128)}, u32[]{:S(2)}, u32[]{:S(2)}) collective-permute-start(f32[2,64,1024]{2,1,0:T(8,128)} %bitcast.131), channel_id=1, source_target_pairs={{1,0},{2,1},{3,2},{4,3},{5,4},{6,5},{7,6},{8,7},{9,8},{10,9},{11,1... | collective-permute-start | bytes 1572872 | tf_op jit(solution)/shard_map/ppermute | solution.py:39
  378.4 71.1 %collective-permute-start.9 = (f32[2,2,64,1024]{3,2,0,1:T(8,128)}, f32[2,2,64,1024]{3,2,0,1:T(8,128)}, u32[]{:S(2)}, u32[]{:S(2)}) collective-permute-start(f32[2,2,64,1024]{3,2,0,1:T(8,128)} %bitcast.128), channel_id=1, source_target_pairs={{0,4},{1,5},{2,6},{3,7},{4,0},{5,1},{6,2},{7,3},{8,12},{9,13},{10,... | collective-permute-start | bytes 3145736 | tf_op jit(solution)/shard_map/ppermute | solution.py:33
  387.2 62.3 %collective-permute-start.7 = (f32[2,2,64,1024]{3,2,0,1:T(8,128)}, f32[2,2,64,1024]{3,2,0,1:T(8,128)}, u32[]{:S(2)}, u32[]{:S(2)}) collective-permute-start(f32[2,2,64,1024]{3,2,0,1:T(8,128)} %bitcast.130), channel_id=1, source_target_pairs={{0,16},{1,17},{2,18},{3,19},{4,20},{5,21},{6,22},{7,23},{8,24},{9,... | collective-permute-start | bytes 3145736 | tf_op jit(solution)/shard_map/ppermute | solution.py:33
  387.2 62.3 %collective-permute-start.8 = (f32[2,2,64,1024]{3,2,0,1:T(8,128)}, f32[2,2,64,1024]{3,2,0,1:T(8,128)}, u32[]{:S(2)}, u32[]{:S(2)}) collective-permute-start(f32[2,2,64,1024]{3,2,0,1:T(8,128)} %bitcast.129), channel_id=1, source_target_pairs={{0,8},{1,9},{2,10},{3,11},{4,12},{5,13},{6,14},{7,15},{8,0},{9,1},... | collective-permute-start | bytes 3145736 | tf_op jit(solution)/shard_map/ppermute | solution.py:33
  401.3 47.0 %collective-permute-start.6 = (f32[2,64,1024]{2,1,0:T(8,128)}, f32[2,64,1024]{2,1,0:T(8,128)}, u32[]{:S(2)}, u32[]{:S(2)}) collective-permute-start(f32[2,64,1024]{2,1,0:T(8,128)} %bitcast.132), channel_id=1, source_target_pairs={{0,1},{1,2},{2,3},{3,4},{4,5},{5,6},{6,7},{7,8},{8,9},{9,10},{10,1... | collective-permute-start | bytes 1572872 | tf_op jit(solution)/shard_map/ppermute | solution.py:39
Sparse Core Ops, SparseCore 0:
  26.4 266.4 all-reduce.5
where the time goes:
time: 461 us; the launch traced here: 459 us
  waiting for transfers between devices  281 us (61%)
  local copies, waits for them, and re-layouts  83.4 us (18%)
  matrix products  33.1 us (7%)
  starting transfers between devices  29.7 us (6%)
  between operations  16.9 us (4%)
  other arithmetic  15.4 us (3%)
    psum x1, waiting for transfers between devices, from_root(): return lax.psum(block, axis)  234 us
    ppermute x2, waiting for transfers between devices, passed_along(): return lax.ppermute(array, axis, pairs)  37.3 us
    another operation x4, local copies, waits for them, and re-layouts, local(): jnp.stack([grad_key, grad_value])  31.5 us
    ppermute x6, starting transfers between devices, partner_2(): lax.ppermute(array, axis, [(i, i ^ 1 << distance) for i in range(lax.axis...  17.7 us
    concatenate x1, local copies, waits for them, and re-layouts, local(): every_key = jnp.concatenate([window, global_part] + random_parts, axis=2)  10.3 us
    ppermute x1, waiting for transfers between devices, padded_2(): before = lax.ppermute(last, axis, up)  9.38 us
  transfers between devices with their start and end apart: 11, of which 3 were waited for; matrix products, arithmetic and copies ran while one was open for 9% of the time, Pallas kernels for 0%

commit v1 on v0

--- a/solution.py
+++ b/solution.py
@@ -26,7 +26,7 @@
 
 def from_root(block, axis, source):
     block = jnp.where(lax.axis_index(axis) == source, block, jnp.zeros_like(block))
-    return lax.psum(block, axis)
+    return jnp.sum(lax.all_gather(block, axis), 0)
 
 
 def partner_2(array, axis, distance):

time: 461 us -> 338 us (0.73)
  the two profiles are of different devices: /device:TPU:96 before, /device:TPU:36 now
where the time goes in v1:
time: 338 us; the launch traced here: 331 us
  waiting for transfers between devices  146 us (43%)
  local copies, waits for them, and re-layouts  84.7 us (25%)
  matrix products  33.2 us (10%)
  other arithmetic  26.7 us (8%)
  starting transfers between devices  23.8 us (7%)
  between operations  17.2 us (5%)
    all_gather x2, waiting for transfers between devices, from_root(): return jnp.sum(lax.all_gather(block, axis), 0)  85.2 us
    ppermute x2, waiting for transfers between devices, passed_along(): return lax.ppermute(array, axis, pairs)  34.1 us
    another operation x4, local copies, waits for them, and re-layouts, local(): jnp.stack([grad_key, grad_value])  31.6 us
    ppermute x1, waiting for transfers between devices, padded_2(): before = lax.ppermute(last, axis, up)  25.8 us
    reduce_sum x2, other arithmetic, from_root(): return jnp.sum(lax.all_gather(block, axis), 0)  11.9 us
    concatenate x1, local copies, waits for them, and re-layouts, local(): every_key = jnp.concatenate([window, global_part] + random_parts, axis=2)  10.3 us
    ppermute x6, starting transfers between devices, partner_2(): lax.ppermute(array, axis, [(i, i ^ 1 << distance) for i in range(lax.axis...  10.1 us
    dot_general x3, matrix products, local(): jnp.einsum('jb,sjqd->sbqd', pickers[matching].astype(jnp.float32), terms,...  8.28 us
  transfers between devices with their start and end apart: 12, of which 4 were waited for; matrix products, arithmetic and copies ran while one was open for 14% of the time, Pallas kernels for 0%

profile of v1, /device:TPU:36, one launch (start us, length us, event | category | flops | bytes accessed | tf_op | source)
XLA Modules:
  0.0 331.3 jit_solution(13053201926568808768)
XLA Ops:
  11.2 2.2 fusion.33
  14.2 1.9 pad_maximum_fusion.2
  16.1 3.2 collective-permute-start.4
  19.3 3.3 collective-permute-start.2
  22.7 1.9 collective-permute-start
  24.6 5.8 %collective-permute-start.1 = (bf16[2,64,1024]{2,1,0:T(8,128)(2,1)S(1)}, bf16[2,64,1024]{2,1,0:T(8,128)(2,1)S(1)}, u32[]{:S(2)}, u32[]{:S(2)}) collective-permute-start(bf16[2,64,1024]{2,1,0:T(8,128)(2,1)S(1)} %get-tuple-element.46), channel_id=1, source_target_pairs={{1,0},{2,1},{3,2},{4,3},{5,4},{6,5},{7,6},{8,7},{9,8},{10,9},{11,1... | collective-permute-start | bytes 786440 | tf_op jit(solution)/shard_map/ppermute | solution.py:22
  30.5 1.3 reshape.131
  35.1 25.8 %collective-permute-done = bf16[2,64,1024]{2,1,0:T(8,128)(2,1)S(1)} collective-permute-done((bf16[2,64,1024]{2,1,0:T(8,128)(2,1)S(1)}, bf16[2,64,1024]{2,1,0:T(8,128)(2,1)S(1)}, u32[]{:S(2)}, u32[]{:S(2)}) %collective-permute-start) | collective-permute-done | bytes 262176 | tf_op jit(solution)/shard_map/ppermute | solution.py:21
  62.9 1.5 copy.105
  64.5 2.6 fusion.15
  67.1 2.7 copy.74
  69.8 2.6 fusion.13
  72.4 2.3 copy.72
  74.8 2.6 fusion.14
  77.4 2.3 copy.73
  79.7 19.3 %all-gather.5.cloned.1.call-done = bf16[64,64,1024]{2,1,0:T(8,128)(2,1)} async-done(((bf16[2,64,1024]{2,1,0:T(8,128)(2,1)}), bf16[64,64,1024]{2,1,0:T(8,128)(2,1)}) %all-gather.5.cloned.1.call-update) | async-done | bytes 8388624 | tf_op jit(solution)/shard_map/all_gather | solution.py:29
  99.0 5.6 %reduce_sum.42 = bf16[2,64,1024]{2,1,0:T(8,128)(2,1)S(1)} reduce(bf16[32,2,64,1024]{3,2,1,0:T(8,128)(2,1)} %bitcast.132, bf16[]{:T(256)} %constant.102.clone.1), dimensions={0}, to_apply=%region_0.1 | reduce | flops 4063232 | bytes 8650754 | tf_op jit(solution)/shard_map/reduce_sum | solution.py:29
  104.5 65.9 %all-gather.7.cloned.1.call-done = bf16[64,64,1024]{2,1,0:T(8,128)(2,1)} async-done(((bf16[2,64,1024]{2,1,0:T(8,128)(2,1)}), bf16[64,64,1024]{2,1,0:T(8,128)(2,1)}) %all-gather.7.cloned.1.call-update) | async-done | bytes 8388624 | tf_op jit(solution)/shard_map/all_gather | solution.py:29
  170.4 6.3 %reduce_sum.43 = bf16[2,64,1024]{2,1,0:T(8,128)(2,1)} reduce(bf16[32,2,64,1024]{3,2,1,0:T(8,128)(2,1)} %bitcast.133, bf16[]{:T(256)} %constant.102.clone.1), dimensions={0}, to_apply=%region_1.2 | reduce | flops 4063232 | bytes 8650754 | tf_op jit(solution)/shard_map/reduce_sum | solution.py:29
  178.6 2.0 copy.65
  180.6 2.2 broadcast_in_dim.25
  182.8 10.3 %concatenate.15 = bf16[2,2,512,1024]{2,3,1,0:T(8,128)(2,1)} concatenate(bf16[2,2,64,1024]{2,3,1,0:T(8,128)(2,1)S(1)} %copy.105, bf16[2,2,64,1024]{2,3,1,0:T(8,128)(2,1)S(1)} %copy.106, bf16[2,2,64,1024]{2,3,1,0:T(8,128)(2,1)S(1)} %copy.107, bf16[2,2,128,1024]{2,3,1,0:T(8,128)(2,1)} %broadcast_in_dim.25, bf16[2,2,64,1024]{2,3,1,0:T(8,128)(2,1)} %copy.72, ...), dimensions={2} | concatenate | bytes 8388608 | tf_op jit(solution)/shard_map/concatenate | solution.py:116
  193.1 4.0 %fusion.49 = (bf16[1,2,512,1024]{2,3,1,0:T(8,128)(2,1)S(1)}, bf16[1,2,512,1024]{2,3,1,0:T(8,128)(2,1)}) fusion(bf16[2,2,512,1024]{2,3,1,0:T(8,128)(2,1)} %concatenate.15), kind=kLoop, calls=%fused_computation.97 | loop fusion | bytes 8388608 | tf_op jit(solution)/shard_map/slice | solution.py:117
  197.1 3.4 %fusion.55 = (f32[2,16,64]{2,1,0:T(8,128)S(1)}, f32[2,16,64,512]{3,2,1,0:T(8,128)}) fusion(pred[2,512]{1,0:T(4,128)(4,1)S(1)} %add_add_fusion, bf16[2,64,16,64]{1,3,2,0:T(8,128)(2,1)S(1)} %copy-done.9, bf16[2,512,16,64]{1,3,2,0:T(8,128)(2,1)S(1)} %bitcast.134), kind=kOutput, calls=%fused_computation.103 | convolution fusion | flops 138412544 | bytes 6562816 | tf_op jit(solution)/shard_map/sub | solution.py:50
  200.5 5.0 %convolution_bitcast_fusion = f32[2,512,16,64]{1,3,2,0:T(8,128)} fusion(bf16[2,64,16,64]{1,3,2,0:T(8,128)(2,1)S(1)} %copy-done.10, f32[2,16,64,512]{3,2,1,0:T(8,128)} %get-tuple-element.55, f32[2,16,64]{2,1,0:T(8,128)S(1)} %get-tuple-element.54), kind=kOutput, calls=%fused_computation.11 | convolution fusion | flops 136314880 | bytes 8658944 | tf_op jit(solution)/shard_map/jhqk,jqhd->jkhd/dot_general | solution.py:68
  207.8 2.6 convolution_bitcast_fusion.1
  210.4 7.1 %reshape.143 = f32[1,2,8,64,1024]{3,2,4,1,0:T(8,128)} reshape(f32[2,512,16,64]{1,3,2,0:T(8,128)} %convolution_bitcast_fusion.1) | data formatting | bytes 8388608 | tf_op jit(solution)/shard_map/stack | solution.py:137
  217.5 8.8 %copy.83 = f32[1,2,8,64,1024]{4,1,3,0,2:T(2,128)} copy(f32[1,2,8,64,1024]{3,2,4,1,0:T(8,128)} %reshape.143) | data formatting | bytes 8388608 | tf_op jit(solution)/shard_map/stack | solution.py:137
  226.3 7.1 %reshape.144 = f32[1,2,8,64,1024]{3,2,4,1,0:T(8,128)} reshape(f32[2,512,16,64]{1,3,2,0:T(8,128)} %convolution_bitcast_fusion) | data formatting | bytes 8388608 | tf_op jit(solution)/shard_map/stack | solution.py:137
  233.4 8.6 %copy.84 = f32[1,2,8,64,1024]{4,1,3,0,2:T(2,128)} copy(f32[1,2,8,64,1024]{3,2,4,1,0:T(8,128)} %reshape.144) | data formatting | bytes 8388608 | tf_op jit(solution)/shard_map/stack | solution.py:137
  242.0 3.6 %fusion.20 = f32[2,64,1024,2]{2,3,1,0:T(2,128)S(1)} fusion(f32[1,2,8,64,1024]{4,1,3,0,2:T(2,128)} %copy.84, f32[1,2,8,64,1024]{4,1,3,0,2:T(2,128)} %copy.83, s32[2]{0:T(128)S(1)} %get-tuple-element.30), kind=kOutput, calls=%fused_computation.43 | convolution fusion | flops 6553604 | bytes 9437192 | tf_op jit(solution)/shard_map/jb,sjqd->sbqd/dot_general | solution.py:151
  245.8 2.3 fusion.19
  248.1 2.3 fusion.21
  250.4 1.9 maximum_bitcast_fusion.4
  253.6 1.3 copy.127
  256.3 1.3 pad_add_fusion
  257.6 2.1 fusion.50
  260.5 4.0 %collective-permute-start.5 = (f32[2,64,1024]{2,1,0:T(8,128)}, f32[2,64,1024]{2,1,0:T(8,128)}, u32[]{:S(2)}, u32[]{:S(2)}) collective-permute-start(f32[2,64,1024]{2,1,0:T(8,128)} %bitcast.130), channel_id=1, source_target_pairs={{1,0},{2,1},{3,2},{4,3},{5,4},{6,5},{7,6},{8,7},{9,8},{10,9},{11,1... | collective-permute-start | bytes 1572872 | tf_op jit(solution)/shard_map/ppermute | solution.py:39
  268.1 1.6 fusion.11
  270.3 2.3 copy.76
  272.5 2.1 convert_element_type.75
  274.7 2.0 copy.129
  276.7 1.9 collective-permute-start.6
  278.6 3.1 fusion.12
  281.7 1.5 copy.78
  284.6 1.3 fusion.24
  285.9 34.1 %collective-permute-done.6 = f32[2,64,1024]{2,1,0:T(8,128)} collective-permute-done((f32[2,64,1024]{2,1,0:T(8,128)}, f32[2,64,1024]{2,1,0:T(8,128)}, u32[]{:S(2)}, u32[]{:S(2)}) %collective-permute-start.6) | collective-permute-done | bytes 524320 | tf_op jit(solution)/shard_map/ppermute | solution.py:39
  321.2 2.2 add_convert_fusion
  (72 shorter events, 22.9 us)
Async XLA Ops:
  7.2 53.7 %copy-start.6 = (bf16[128,1024]{1,0:T(8,128)(2,1)S(1)}, bf16[128,1024]{1,0:T(8,128)(2,1)}, u32[]{:S(2)}) copy-start(bf16[128,1024]{1,0:T(8,128)(2,1)} %param.12) | copy-start | bytes 786436
  7.2 53.7 %copy-start.5 = (bf16[128,1024]{1,0:T(8,128)(2,1)S(1)}, bf16[128,1024]{1,0:T(8,128)(2,1)}, u32[]{:S(2)}) copy-start(bf16[128,1024]{1,0:T(8,128)(2,1)} %param.11) | copy-start | bytes 786436
  7.2 25.9 %copy-start.11 = (bf16[128,1024]{1,0:T(8,128)(2,1)S(1)}, bf16[128,1024]{1,0:T(8,128)(2,1)}, u32[]{:S(2)}) copy-start(bf16[128,1024]{1,0:T(8,128)(2,1)} %param.13) | copy-start | bytes 786436
  7.2 27.7 %copy-start.12 = (s32[2,3]{1,0:T(2,128)S(1)}, s32[2,3]{1,0:T(2,128)}, u32[]{:S(2)}) copy-start(s32[2,3]{1,0:T(2,128)} %param.14) | copy-start | bytes 76
  7.2 91.8 %all-gather.5.cloned.1.call-start = ((), (), s32[]{:S(2)}) async-start(), calls=%async_computation | async-start | bytes 8650752 | tf_op jit(solution)/shard_map/all_gather | solution.py:29
  13.4 157.0 %all-gather.7.cloned.1.call-start = ((), (), s32[]{:S(2)}) async-start(), calls=%async_computation.1 | async-start | bytes 8650752 | tf_op jit(solution)/shard_map/all_gather | solution.py:29
  16.1 48.4 %collective-permute-start.4 = (bf16[2,128,1024]{2,1,0:T(8,128)(2,1)}, bf16[2,128,1024]{2,1,0:T(8,128)(2,1)}, u32[]{:S(2)}, u32[]{:S(2)}) collective-permute-start(bf16[2,128,1024]{2,1,0:T(8,128)(2,1)} %pad_maximum_fusion.2), channel_id=1, source_target_pairs={{0,4},{1,5},{2,6},{3,7},{4,0},{5,1},{6,2},{7,3},{8,12},{9,13},{10,... | collective-permute-start | bytes 1572872 | tf_op jit(solution)/shard_map/ppermute | solution.py:33
  19.3 50.6 %collective-permute-start.2 = (bf16[2,128,1024]{2,1,0:T(8,128)(2,1)}, bf16[2,128,1024]{2,1,0:T(8,128)(2,1)}, u32[]{:S(2)}, u32[]{:S(2)}) collective-permute-start(bf16[2,128,1024]{2,1,0:T(8,128)(2,1)} %pad_maximum_fusion.2), channel_id=1, source_target_pairs={{0,16},{1,17},{2,18},{3,19},{4,20},{5,21},{6,22},{7,23},{8,24},{9,... | collective-permute-start | bytes 1572872 | tf_op jit(solution)/shard_map/ppermute | solution.py:33
  22.6 52.2 %collective-permute-start.3 = (bf16[2,128,1024]{2,1,0:T(8,128)(2,1)}, bf16[2,128,1024]{2,1,0:T(8,128)(2,1)}, u32[]{:S(2)}, u32[]{:S(2)}) collective-permute-start(bf16[2,128,1024]{2,1,0:T(8,128)(2,1)} %pad_maximum_fusion.2), channel_id=1, source_target_pairs={{0,8},{1,9},{2,10},{3,11},{4,12},{5,13},{6,14},{7,15},{8,0},{9,1},... | collective-permute-start | bytes 1572872 | tf_op jit(solution)/shard_map/ppermute | solution.py:33
  22.7 38.2 %collective-permute-start = (bf16[2,64,1024]{2,1,0:T(8,128)(2,1)S(1)}, bf16[2,64,1024]{2,1,0:T(8,128)(2,1)S(1)}, u32[]{:S(2)}, u32[]{:S(2)}) collective-permute-start(bf16[2,64,1024]{2,1,0:T(8,128)(2,1)S(1)} %get-tuple-element.45), channel_id=1, source_target_pairs={{0,1},{1,2},{2,3},{3,4},{4,5},{5,6},{6,7},{7,8},{8,9},{9,10},{10,1... | collective-permute-start | bytes 786440 | tf_op jit(solution)/shard_map/ppermute | solution.py:21
  24.6 36.3 %collective-permute-start.1 = (bf16[2,64,1024]{2,1,0:T(8,128)(2,1)S(1)}, bf16[2,64,1024]{2,1,0:T(8,128)(2,1)S(1)}, u32[]{:S(2)}, u32[]{:S(2)}) collective-permute-start(bf16[2,64,1024]{2,1,0:T(8,128)(2,1)S(1)} %get-tuple-element.46), channel_id=1, source_target_pairs={{1,0},{2,1},{3,2},{4,3},{5,4},{6,5},{7,6},{8,7},{9,8},{10,9},{11,1... | collective-permute-start | bytes 786440 | tf_op jit(solution)/shard_map/ppermute | solution.py:22
  193.1 4.0 %copy-start.9 = (bf16[2,64,16,64]{1,3,2,0:T(8,128)(2,1)S(1)}, bf16[2,64,16,64]{1,3,2,0:T(8,128)(2,1)}, u32[]{:S(2)}) copy-start(bf16[2,64,16,64]{1,3,2,0:T(8,128)(2,1)} %copy.79) | copy-start | bytes 786436
  197.1 8.4 %copy-start.2 = (bf16[1,2,512,1024]{2,3,1,0:T(8,128)(2,1)}, bf16[1,2,512,1024]{2,3,1,0:T(8,128)(2,1)S(1)}, u32[]{:S(2)}) copy-start(bf16[1,2,512,1024]{2,3,1,0:T(8,128)(2,1)S(1)} %get-tuple-element.34) | copy-start | bytes 6291460
  197.1 3.4 %copy-start.10 = (bf16[2,64,16,64]{1,3,2,0:T(8,128)(2,1)S(1)}, bf16[2,64,16,64]{1,3,2,0:T(8,128)(2,1)}, u32[]{:S(2)}) copy-start(bf16[2,64,16,64]{1,3,2,0:T(8,128)(2,1)} %copy.81) | copy-start | bytes 786436
  200.5 5.0 %copy-start.3 = (f32[2,16,64,512]{3,2,1,0:T(8,128)S(1)}, f32[2,16,64,512]{3,2,1,0:T(8,128)}, u32[]{:S(2)}) copy-start(f32[2,16,64,512]{3,2,1,0:T(8,128)} %get-tuple-element.55) | copy-start | bytes 12582916
  200.5 5.0 %copy-start.7 = (bf16[1,2,512,1024]{2,3,1,0:T(8,128)(2,1)S(1)}, bf16[1,2,512,1024]{2,3,1,0:T(8,128)(2,1)}, u32[]{:S(2)}) copy-start(bf16[1,2,512,1024]{2,3,1,0:T(8,128)(2,1)} %get-tuple-element.35) | copy-start | bytes 6291460
  242.0 3.6 %copy-start = (f32[1,2,8,64,1024]{4,1,3,0,2:T(2,128)S(1)}, f32[1,2,8,64,1024]{4,1,3,0,2:T(2,128)}, u32[]{:S(2)}) copy-start(f32[1,2,8,64,1024]{4,1,3,0,2:T(2,128)} %copy.83) | copy-start | bytes 12582916
  242.0 3.8 %copy-start.1 = (f32[1,2,8,64,1024]{4,1,3,0,2:T(2,128)S(1)}, f32[1,2,8,64,1024]{4,1,3,0,2:T(2,128)}, u32[]{:S(2)}) copy-start(f32[1,2,8,64,1024]{4,1,3,0,2:T(2,128)} %copy.84) | copy-start | bytes 12582916
  256.2 11.9 %copy-start.4 = (f32[2,16,64,512]{3,2,1,0:T(8,128)S(1)}, f32[2,16,64,512]{3,2,1,0:T(8,128)}, u32[]{:S(2)}) copy-start(f32[2,16,64,512]{3,2,1,0:T(8,128)} %get-tuple-element.55) | copy-start | bytes 12582916
  256.2 11.9 %copy-start.8 = (bf16[1,2,512,1024]{2,3,1,0:T(8,128)(2,1)S(1)}, bf16[1,2,512,1024]{2,3,1,0:T(8,128)(2,1)}, u32[]{:S(2)}) copy-start(bf16[1,2,512,1024]{2,3,1,0:T(8,128)(2,1)} %get-tuple-element.35) | copy-start | bytes 6291460
  260.5 24.0 %collective-permute-start.5 = (f32[2,64,1024]{2,1,0:T(8,128)}, f32[2,64,1024]{2,1,0:T(8,128)}, u32[]{:S(2)}, u32[]{:S(2)}) collective-permute-start(f32[2,64,1024]{2,1,0:T(8,128)} %bitcast.130), channel_id=1, source_target_pairs={{1,0},{2,1},{3,2},{4,3},{5,4},{6,5},{7,6},{8,7},{9,8},{10,9},{11,1... | collective-permute-start | bytes 1572872 | tf_op jit(solution)/shard_map/ppermute | solution.py:39
  264.5 56.7 %collective-permute-start.9 = (f32[2,2,64,1024]{3,2,0,1:T(8,128)}, f32[2,2,64,1024]{3,2,0,1:T(8,128)}, u32[]{:S(2)}, u32[]{:S(2)}) collective-permute-start(f32[2,2,64,1024]{3,2,0,1:T(8,128)} %bitcast.127), channel_id=1, source_target_pairs={{0,4},{1,5},{2,6},{3,7},{4,0},{5,1},{6,2},{7,3},{8,12},{9,13},{10,... | collective-permute-start | bytes 3145736 | tf_op jit(solution)/shard_map/ppermute | solution.py:33
  265.6 55.7 %collective-permute-start.7 = (f32[2,2,64,1024]{3,2,0,1:T(8,128)}, f32[2,2,64,1024]{3,2,0,1:T(8,128)}, u32[]{:S(2)}, u32[]{:S(2)}) collective-permute-start(f32[2,2,64,1024]{3,2,0,1:T(8,128)} %bitcast.129), channel_id=1, source_target_pairs={{0,16},{1,17},{2,18},{3,19},{4,20},{5,21},{6,22},{7,23},{8,24},{9,... | collective-permute-start | bytes 3145736 | tf_op jit(solution)/shard_map/ppermute | solution.py:33
  266.8 54.4 %collective-permute-start.8 = (f32[2,2,64,1024]{3,2,0,1:T(8,128)}, f32[2,2,64,1024]{3,2,0,1:T(8,128)}, u32[]{:S(2)}, u32[]{:S(2)}) collective-permute-start(f32[2,2,64,1024]{3,2,0,1:T(8,128)} %bitcast.128), channel_id=1, source_target_pairs={{0,8},{1,9},{2,10},{3,11},{4,12},{5,13},{6,14},{7,15},{8,0},{9,1},... | collective-permute-start | bytes 3145736 | tf_op jit(solution)/shard_map/ppermute | solution.py:33
  276.7 43.4 %collective-permute-start.6 = (f32[2,64,1024]{2,1,0:T(8,128)}, f32[2,64,1024]{2,1,0:T(8,128)}, u32[]{:S(2)}, u32[]{:S(2)}) collective-permute-start(f32[2,64,1024]{2,1,0:T(8,128)} %bitcast.131), channel_id=1, source_target_pairs={{0,1},{1,2},{2,3},{3,4},{4,5},{5,6},{6,7},{7,8},{8,9},{9,10},{10,1... | collective-permute-start | bytes 1572872 | tf_op jit(solution)/shard_map/ppermute | solution.py:39
Sparse Core Ops, SparseCore 0:
  13.6 85.3 all-gather.4
  101.4 68.9 all-gather.6
